TPU v7x, 32 devices: a whole 2x2x4 slice. The times are simulated.
32 devices in a mesh: dp: 4 (over y, x), expert: 8 (over z, core).
Axes of the slice: x: 2, y: 2, z: 4, core: 2. Of those that a mesh axis runs over, the one named last changes fastest.
Arguments:
- context: bfloat16 [8, 4, 128, 1536], P('expert', None, None, 'dp'), may hold values from -0.29882812 to 0.29882812
- w_proj: bfloat16 [1536, 1536], P('dp'), may hold values from -0.15625 to 0.15625
- residual: bfloat16 [4096, 1536], P(('dp', 'expert')), may hold values from -0.29882812 to 0.29882812
- gain_first: float32 [1536], replicated, may hold values from 0.25 to 1.75
- gain_next: float32 [1536], replicated, may hold values from 0.25 to 1.75
- w_router: bfloat16 [1536, 40], replicated, may hold values from -0.15625 to 0.15625
- expert_ids: int32 [4096, 8], P(('dp', 'expert')), may hold values from 0 to 39, all different within a row
- replica_pick: int32 [4096, 8], P(('dp', 'expert')), may hold values from 0 to 5039
- slot_expert: int32 [48], replicated, may hold values from 0 to 39, as said below
- cap_blocks: int32 [48], replicated, may hold values from 1 to 4
- w_in: bfloat16 [48, 1536, 1024], P('expert', 'dp'), as said below
- w_out: bfloat16 [48, 512, 1536], P('expert', 'dp'), as said below
Outputs:
- residual_out: bfloat16 [4096, 1536], P(('dp', 'expert'))
- next_normed: bfloat16 [4096, 1536], P(('dp', 'expert'))
Inputs may be any that keep to these rules, and one draw needn't show every extreme that they name: `slot_expert`: every expert is held by at least one slot; slot s lies on index s // 6 of the expert axis. `w_in`: two slots that hold the same expert have equal weights. `w_out`: two slots that hold the same expert have equal weights.
All inputs are finite; a program needn't handle non-finite values.
Results may differ from a plain program's by a relative error of at most 0.01.
Values may be sent and summed in bfloat16 or wider, within the bound.
No kernel may reach another device: no remote copies, remote signals or barrier semaphores. Data moves between devices by JAX's collectives and lax.ppermute only.
A program may use at most 128 MiB of HBM per device.

v0:
```python
import math
import jax
import jax.numpy as jnp
from jax import lax
from jax.sharding import PartitionSpec as P

CAP_UNIT = 8
CAP_MOST = 32


def rms_scale(values, gain):
    widened = values.astype(jnp.float32)
    return widened * lax.rsqrt(jnp.mean(widened * widened, axis=-1, keepdims=True) + 1e-06) * gain


def route_rows(normed, w_router, expert_ids, replica_pick, slot_expert, cap_blocks, cap_unit):
    blocks, row_count, topk_all = expert_ids.shape
    experts_all = w_router.shape[1]
    slots_all = slot_expert.shape[0]
    logits = jnp.dot(normed, w_router, preferred_element_type=jnp.float32)
    logits = logits.reshape(blocks, row_count, experts_all)
    expert_axis = jnp.arange(experts_all)
    one_hot = expert_ids[..., None] == expert_axis
    chosen = jnp.sum(jnp.where(one_hot, logits[:, :, None, :], jnp.float32(0.0)), axis=-1)
    raised = jnp.exp(chosen)
    gates = raised / jnp.sum(raised, axis=-1, keepdims=True)
    holder = (slot_expert[None, :] == expert_axis[:, None]).astype(jnp.int32)
    rep_count = jnp.sum(holder, axis=1)
    earlier = jnp.cumsum(holder, axis=1) - holder
    slot_rank = jnp.sum(earlier * holder, axis=0)
    count_of = jnp.sum(jnp.where(one_hot, rep_count, 0), axis=-1)
    replica = replica_pick % count_of
    slot_axis = jnp.arange(slots_all)
    matched = (slot_expert == expert_ids[..., None]) & (slot_rank == replica[..., None])
    target_slot = jnp.sum(jnp.where(matched, slot_axis, 0), axis=-1)
    flat_count = row_count * topk_all
    selected = matched.reshape(blocks, flat_count, slots_all)
    flat_axis = lax.optimization_barrier(jnp.arange(flat_count))
    lower = (flat_axis[:, None] > flat_axis[None, :]).astype(jnp.bfloat16)
    before = jnp.einsum(
        "ij,bjs->bis", lower, selected.astype(jnp.bfloat16), preferred_element_type=jnp.float32
    )
    position = (
        jnp.sum(jnp.where(selected, before, jnp.float32(0.0)), axis=-1)
        .astype(jnp.int32)
        .reshape(blocks, row_count, topk_all)
    )
    capacity = (
        jnp.sum(jnp.where(target_slot[..., None] == slot_axis, cap_blocks, 0), axis=-1) * cap_unit
    )
    retained = position < capacity
    return (gates, target_slot, position, retained)


def unit_plan(slot_local, n_dp, hidden_units):
    full = slot_local // n_dp
    rest = slot_local - full * n_dp
    chunks = n_dp // math.gcd(rest, n_dp) if rest else 1
    halves = rest * chunks // n_dp
    chunk_width = hidden_units // chunks
    owned_full = [[o * full + j for j in range(full)] for o in range(n_dp)]
    owned_part = [
        [
            (full * n_dp + (o * halves + i) // chunks, (o * halves + i) % chunks)
            for i in range(halves)
        ]
        for o in range(n_dp)
    ]
    return (full, halves, chunks, chunk_width, owned_full, owned_part)


def on_device(
    context,
    w_proj,
    residual,
    gain_first,
    gain_next,
    w_router,
    expert_ids,
    replica_pick,
    slot_expert,
    cap_blocks,
    w_in,
    w_out,
):
    tok_rows, model_width = residual.shape
    topk_all = expert_ids.shape[1]
    slot_local, d_local, _ = w_in.shape
    hidden_units = w_in.shape[2] // 2
    ff_local = w_out.shape[1]
    n_dp = lax.axis_size("dp")
    n_exp = lax.axis_size("expert")
    dp_at = lax.axis_index("dp")
    exp_at = lax.axis_index("expert")
    full, halves, chunks, chunk_width, owned_full, owned_part = unit_plan(
        slot_local, n_dp, hidden_units
    )
    sources_per_chunk = chunk_width // ff_local
    lane_width = 2 * chunk_width if ff_local * model_width % (2 * chunk_width) == 0 else 128

    def as_rows(piece):
        return piece.reshape(-1, lane_width)

    weight_parts = []
    for o in range(n_dp):
        pieces = []
        for s in owned_full[o]:
            pieces += [as_rows(w_in[s]), as_rows(w_out[s])]
        for s, c in owned_part[o]:
            lo = c * chunk_width
            pieces += [
                as_rows(w_in[s, :, lo : lo + chunk_width]),
                as_rows(w_in[s, :, hidden_units + lo : hidden_units + lo + chunk_width]),
                as_rows(w_out[s]),
            ]
        weight_parts.append(jnp.concatenate(pieces, axis=0))
    weight_recv = lax.all_to_all(jnp.stack(weight_parts), "dp", 0, 0, tiled=True)
    offset = 0

    def take(shape):
        nonlocal offset
        count = math.prod(shape) // lane_width
        piece = weight_recv[:, offset : offset + count].reshape((n_dp,) + shape)
        offset += count
        return piece

    full_in, full_out, part_in, part_out = ([], [], [], [])
    for _ in range(full):
        full_in.append(take((d_local, 2 * hidden_units)).reshape(n_dp * d_local, 2 * hidden_units))
        full_out.append(take((ff_local, model_width)).reshape(n_dp * ff_local, model_width))
    for _ in range(halves):
        gate_in = take((d_local, chunk_width))
        up_in = take((d_local, chunk_width))
        part_in.append(
            jnp.concatenate([gate_in, up_in], axis=-1).reshape(n_dp * d_local, 2 * chunk_width)
        )
        part_out.append(take((ff_local, model_width)))
    ids_all = lax.all_gather(
        jnp.concatenate([expert_ids, replica_pick], axis=1), "expert", axis=0, tiled=True
    ).reshape(n_exp, tok_rows, 2 * topk_all)
    flat_context = context.reshape(-1, context.shape[3])
    attended = lax.psum_scatter(
        jnp.dot(flat_context, w_proj, preferred_element_type=jnp.float32).astype(jnp.bfloat16),
        "dp",
        scatter_dimension=0,
        tiled=True,
    )
    hidden_state = (residual.astype(jnp.float32) + attended.astype(jnp.float32)).astype(
        jnp.bfloat16
    )
    normed = rms_scale(hidden_state, gain_first).astype(jnp.bfloat16)
    normed_all = lax.all_gather(normed, "expert", axis=0, tiled=True)
    gates, target_slot, position, retained = route_rows(
        normed_all,
        w_router,
        ids_all[:, :, :topk_all],
        ids_all[:, :, topk_all:],
        slot_expert,
        cap_blocks,
        CAP_UNIT,
    )
    here = retained & (target_slot // slot_local == exp_at)
    local = jnp.where(here, target_slot % slot_local * CAP_MOST + position, -1)
    hit = local[..., None] == jnp.arange(slot_local * CAP_MOST)
    pick = jnp.any(hit, axis=2).astype(jnp.bfloat16)
    weight = jnp.sum(jnp.where(hit, gates[..., None], jnp.float32(0.0)), axis=2)
    slot_in = jnp.einsum(
        "btr,btd->brd",
        pick,
        normed_all.reshape(n_exp, tok_rows, model_width),
        preferred_element_type=jnp.float32,
    ).astype(jnp.bfloat16)
    slot_in = slot_in.reshape(n_exp, slot_local, CAP_MOST, model_width)
    x_parts = []
    for o in range(n_dp):
        x_parts.append(
            jnp.stack(
                [slot_in[:, s] for s in owned_full[o]] + [slot_in[:, s] for s, _ in owned_part[o]]
            )
        )
    x_recv = lax.all_to_all(jnp.stack(x_parts), "dp", 0, 0, tiled=True)
    unit_rows = n_dp * n_exp * CAP_MOST

    def expert_rows(rows, w_up, w_down, width):
        gate_up = jnp.dot(rows, w_up, preferred_element_type=jnp.float32)
        activated = (jax.nn.silu(gate_up[:, :width]) * gate_up[:, width:]).astype(jnp.bfloat16)
        return jnp.dot(activated, w_down, preferred_element_type=jnp.float32).astype(jnp.bfloat16)

    outs = []
    for j in range(full):
        rows = x_recv[:, j].reshape(unit_rows, model_width)
        outs.append(expert_rows(rows, full_in[j], full_out[j], hidden_units))
    for i in range(halves):
        rows = x_recv[:, full + i].reshape(unit_rows, model_width)
        chunk_at = (dp_at * halves + i) % chunks
        w_down = lax.dynamic_slice_in_dim(
            part_out[i], chunk_at * sources_per_chunk, sources_per_chunk, axis=0
        ).reshape(chunk_width, model_width)
        outs.append(expert_rows(rows, part_in[i], w_down, chunk_width))
    y_send = (
        jnp.stack(outs)
        .reshape(full + halves, n_dp, n_exp, CAP_MOST, model_width)
        .transpose(1, 0, 2, 3, 4)
    )
    y_recv = lax.all_to_all(y_send, "dp", 0, 0, tiled=True)
    slot_out = [None] * slot_local
    for o in range(n_dp):
        for j, s in enumerate(owned_full[o]):
            slot_out[s] = y_recv[o, j]
        for i, (s, _) in enumerate(owned_part[o]):
            part = y_recv[o, full + i].astype(jnp.float32)
            slot_out[s] = part if slot_out[s] is None else slot_out[s] + part
    slot_out = [part.astype(jnp.bfloat16) for part in slot_out]
    expert_out = (
        jnp.stack(slot_out, axis=1)
        .reshape(n_exp, slot_local * CAP_MOST, model_width)
        .astype(jnp.bfloat16)
    )
    weight_hi = weight.astype(jnp.bfloat16)
    weight_lo = (weight - weight_hi.astype(jnp.float32)).astype(jnp.bfloat16)
    partial = jnp.einsum(
        "btr,brd->btd", weight_hi, expert_out, preferred_element_type=jnp.float32
    ) + jnp.einsum("btr,brd->btd", weight_lo, expert_out, preferred_element_type=jnp.float32)
    combined = lax.psum_scatter(
        partial.reshape(n_exp * tok_rows, model_width), "expert", scatter_dimension=0, tiled=True
    )
    residual_out = (hidden_state.astype(jnp.float32) + combined.astype(jnp.float32)).astype(
        jnp.bfloat16
    )
    next_normed = rms_scale(residual_out, gain_next).astype(jnp.bfloat16)
    return (residual_out, next_normed)


def solution(mesh):
    placed = (
        P("expert", None, None, "dp"),
        P("dp", None),
        P(("dp", "expert"), None),
        P(),
        P(),
        P(),
        P(("dp", "expert"), None),
        P(("dp", "expert"), None),
        P(),
        P(),
        P("expert", "dp", None),
        P("expert", "dp", None),
    )
    return jax.shard_map(
        on_device,
        mesh=mesh,
        in_specs=placed,
        out_specs=(P(("dp", "expert"), None), P(("dp", "expert"), None)),
        check_vma=False,
    )
```

profile of v0, /device:TPU:0, one launch (start us, length us, event | category | flops | bytes accessed | tf_op | source)
XLA Modules:
  0.0 409.4 jit_solution(10336887826829885044)
XLA Ops:
  8.4 3.1 convolution_convert_fusion.3
  11.7 2.3 fusion.60
  31.1 2.2 fusion.61
  42.9 2.7 reduce-scatter.3.cloned.1.call-done
  54.2 6.1 %pad_maximum_fusion = bf16[4,1920,512]{2,1,0:T(8,128)(2,1)} fusion(bf16[1,1920,512]{2,1,0:T(8,128)(2,1)} %bitcast.19, bf16[1,1920,512]{2,1,0:T(8,128)(2,1)} %bitcast.18, bf16[1,1920,512]{2,1,0:T(8,128)(2,1)S(1)} %bitcast.110, bf16[1,1920,512]{2,1,0:T(8,128)(2,1)S(1)} %bitcast.111), kind=kLoop, calls=%fused_computation | loop fusion | flops 11796480 | bytes 15728640 | tf_op jit(solution)/shard_map/stack | solution.py:117
  60.3 5.7 %all-to-all-start.1 = ((bf16[4,1920,512]{2,1,0:T(8,128)(2,1)}), bf16[4,1920,512]{2,1,0:T(8,128)(2,1)}, u32[]{:S(2)}, u32[]{:S(2)}) async-start(bf16[4,1920,512]{2,1,0:T(8,128)(2,1)} %pad_maximum_fusion), calls=%async_computation.2 | async-start | bytes 15728640 | tf_op jit(solution)/shard_map/all_to_all | solution.py:117
  66.0 14.7 %all_gather.6 = s32[1024,16]{0,1:T(8,128)S(1)} all-gather(s32[128,16]{0,1:T(8,128)S(1)} %pad_add_fusion), channel_id=1, replica_groups=mesh['dp'=4,'expert'=8] {'expert'}, dimensions={0}, use_global_device_ids=true | all-gather | bytes 73728 | tf_op jit(solution)/shard_map/all_gather | solution.py:138
  87.7 3.3 convolution_convert_fusion
  92.0 3.5 pad_maximum_fusion.1
  95.5 57.2 %all-to-all-done.1 = bf16[4,1920,512]{2,1,0:T(8,128)(2,1)} async-done(((bf16[4,1920,512]{2,1,0:T(8,128)(2,1)}), bf16[4,1920,512]{2,1,0:T(8,128)(2,1)}, u32[]{:S(2)}, u32[]{:S(2)}) %all-to-all-start.1) | async-done | bytes 7864352 | tf_op jit(solution)/shard_map/all_to_all | solution.py:117
  152.8 5.5 %all-to-all-start = ((bf16[4,2,8,32,1536]{4,3,2,1,0:T(8,128)(2,1)}), bf16[4,2,8,32,1536]{4,3,2,1,0:T(8,128)(2,1)}, u32[]{:S(2)}, u32[]{:S(2)}) async-start(bf16[4,2,8,32,1536]{4,3,2,1,0:T(8,128)(2,1)} %pad_maximum_fusion.1), calls=%async_computation.1 | async-start | bytes 12582912 | tf_op jit(solution)/shard_map/all_to_all | solution.py:181
  162.2 3.4 fusion.57
  165.6 3.7 reshape_reshape.7
  169.3 3.8 slice.193
  173.1 5.7 %reshape_reshape.6 = bf16[1536,1024]{1,0:T(8,128)(2,1)} reshape(bf16[4,768,512]{2,1,0:T(8,128)(2,1)} %slice.193) | data formatting | bytes 6291456 | tf_op jit(solution)/shard_map/reshape;reshape | solution.py:129
  181.6 45.9 %all-to-all-done = bf16[4,2,8,32,1536]{4,3,2,1,0:T(8,128)(2,1)} async-done(((bf16[4,2,8,32,1536]{4,3,2,1,0:T(8,128)(2,1)}), bf16[4,2,8,32,1536]{4,3,2,1,0:T(8,128)(2,1)}, u32[]{:S(2)}, u32[]{:S(2)}) %all-to-all-start) | async-done | bytes 6291488 | tf_op jit(solution)/shard_map/all_to_all | solution.py:181
  227.5 3.4 fusion.59
  231.2 3.4 fusion.64
  239.3 3.2 maximum_bitcast_fusion
  242.5 5.4 %all-to-all-start.2 = ((bf16[4,2,8,32,1536]{4,3,2,1,0:T(8,128)(2,1)}), bf16[4,2,8,32,1536]{4,3,2,1,0:T(8,128)(2,1)}, u32[]{:S(2)}, u32[]{:S(2)}) async-start(bf16[4,2,8,32,1536]{4,3,2,1,0:T(8,128)(2,1)} %maximum_bitcast_fusion), calls=%async_computation.3 | async-start | bytes 12582912 | tf_op jit(solution)/shard_map/all_to_all | solution.py:205
  248.2 2.9 convolution_bitcast_fusion
  252.6 64.7 %all-to-all-done.2 = bf16[4,2,8,32,1536]{4,3,2,1,0:T(8,128)(2,1)} async-done(((bf16[4,2,8,32,1536]{4,3,2,1,0:T(8,128)(2,1)}), bf16[4,2,8,32,1536]{4,3,2,1,0:T(8,128)(2,1)}, u32[]{:S(2)}, u32[]{:S(2)}) %all-to-all-start.2) | async-done | bytes 6291488 | tf_op jit(solution)/shard_map/all_to_all | solution.py:205
  326.8 3.7 convolution_add_fusion
  330.6 69.9 %reduce-scatter.5.cloned.1.call-done = f32[128,1536]{1,0:T(8,128)} async-done(((f32[1024,1536]{1,0:T(8,128)}), f32[128,1536]{1,0:T(8,128)}) %reduce-scatter.5.cloned.1.call-update) | async-done | bytes 786448 | tf_op jit(solution)/shard_map/reduce_scatter | solution.py:224
  (157 shorter events, 69.4 us)
Async XLA Ops:
  7.2 38.5 %reduce-scatter.3.cloned.1.call-start = ((), (), s32[]{:S(2)}) async-start(), calls=%async_computation.5 | async-start | bytes 1966080 | tf_op jit(solution)/shard_map/reduce_scatter | solution.py:142
  11.6 76.1 %all-gather.2.cloned.1.call-start = ((), (), s32[]{:S(2)}) async-start(), calls=%async_computation.6 | async-start | bytes 3538944 | tf_op jit(solution)/shard_map/all_gather | solution.py:152
  14.0 8.0 %copy-start.8 = (bf16[6,128,1536]{2,1,0:T(8,128)(2,1)S(1)}, bf16[6,128,1536]{2,1,0:T(8,128)(2,1)}, u32[]{:S(2)}) copy-start(bf16[6,128,1536]{2,1,0:T(8,128)(2,1)} %param.23) | copy-start | bytes 7077892
  23.1 5.1 %copy-start.13 = (bf16[1,128,1536]{2,1,0:T(8,128)(2,1)S(1)}, bf16[1,128,1536]{2,1,0:T(8,128)(2,1)}, u32[]{:S(2)}) copy-start(bf16[1,128,1536]{2,1,0:T(8,128)(2,1)} %get-tuple-element.33) | copy-start | bytes 1179652
  39.4 2.7 copy-start.11
  40.3 5.3 %copy-start.2 = (bf16[128,1536]{1,0:T(8,128)(2,1)S(1)}, bf16[128,1536]{1,0:T(8,128)(2,1)}, u32[]{:S(2)}) copy-start(bf16[128,1536]{1,0:T(8,128)(2,1)} %param.14) | copy-start | bytes 1179652
  40.4 6.5 %copy-start.26 = (f32[1536]{0:T(1024)S(1)}, f32[1536]{0:T(1024)}, u32[]{:S(2)}) copy-start(f32[1536]{0:T(1024)} %param.15) | copy-start | bytes 18436
  42.1 10.1 %copy-start.5 = (bf16[768,512]{1,0:T(8,128)(2,1)S(1)}, bf16[768,512]{1,0:T(8,128)(2,1)}, u32[]{:S(2)}) copy-start(bf16[768,512]{1,0:T(8,128)(2,1)} %reshape_squeeze.63) | copy-start | bytes 2359300
  48.8 3.5 copy-start.19
  48.8 3.5 copy-start.23
  48.8 3.5 copy-start.24
  60.3 5.7 %copy-start.29 = (s32[128,8]{0,1:T(8,128)S(1)}, s32[128,8]{0,1:T(8,128)}, u32[]{:S(2)}) copy-start(s32[128,8]{0,1:T(8,128)} %param.19) | copy-start | bytes 12292
  60.3 5.7 %copy-start.30 = (s32[128,8]{0,1:T(8,128)S(1)}, s32[128,8]{0,1:T(8,128)}, u32[]{:S(2)}) copy-start(s32[128,8]{0,1:T(8,128)} %param.18) | copy-start | bytes 12292
  60.3 20.7 %copy-start.28 = (s32[48]{0:T(128)S(1)}, s32[48]{0:T(128)}, u32[]{:S(2)}) copy-start(s32[48]{0:T(128)} %param.20) | copy-start | bytes 580
  60.3 92.5 %all-to-all-start.1 = ((bf16[4,1920,512]{2,1,0:T(8,128)(2,1)}), bf16[4,1920,512]{2,1,0:T(8,128)(2,1)}, u32[]{:S(2)}, u32[]{:S(2)}) async-start(bf16[4,1920,512]{2,1,0:T(8,128)(2,1)} %pad_maximum_fusion), calls=%async_computation.2 | async-start | bytes 15728640 | tf_op jit(solution)/shard_map/all_to_all | solution.py:117
  152.8 74.7 %all-to-all-start = ((bf16[4,2,8,32,1536]{4,3,2,1,0:T(8,128)(2,1)}), bf16[4,2,8,32,1536]{4,3,2,1,0:T(8,128)(2,1)}, u32[]{:S(2)}, u32[]{:S(2)}) async-start(bf16[4,2,8,32,1536]{4,3,2,1,0:T(8,128)(2,1)} %pad_maximum_fusion.1), calls=%async_computation.1 | async-start | bytes 12582912 | tf_op jit(solution)/shard_map/all_to_all | solution.py:181
  227.5 3.7 copy-start.4
  231.2 3.4 copy-start.9
  242.5 5.7 %copy-start.25 = (bf16[1536,40]{0,1:T(8,128)(2,1)S(1)}, bf16[1536,40]{0,1:T(8,128)(2,1)}, u32[]{:S(2)}) copy-start(bf16[1536,40]{0,1:T(8,128)(2,1)} %param.17) | copy-start | bytes 368644
  242.5 74.8 %all-to-all-start.2 = ((bf16[4,2,8,32,1536]{4,3,2,1,0:T(8,128)(2,1)}), bf16[4,2,8,32,1536]{4,3,2,1,0:T(8,128)(2,1)}, u32[]{:S(2)}, u32[]{:S(2)}) async-start(bf16[4,2,8,32,1536]{4,3,2,1,0:T(8,128)(2,1)} %maximum_bitcast_fusion), calls=%async_computation.3 | async-start | bytes 12582912 | tf_op jit(solution)/shard_map/all_to_all | solution.py:205
  247.9 152.6 %reduce-scatter.5.cloned.1.call-start = ((), (), s32[]{:S(2)}) async-start(), calls=%async_computation.7 | async-start | bytes 7077888 | tf_op jit(solution)/shard_map/reduce_scatter | solution.py:224
  330.5 70.0 %copy-start.3 = (bf16[128,1536]{1,0:T(8,128)(2,1)S(1)}, bf16[128,1536]{1,0:T(8,128)(2,1)}, u32[]{:S(2)}) copy-start(bf16[128,1536]{1,0:T(8,128)(2,1)} %reduce-scatter.3.cloned.1.call-done) | copy-start | bytes 1179652
  330.6 71.3 %copy-start.27 = (f32[1536]{0:T(1024)S(1)}, f32[1536]{0:T(1024)}, u32[]{:S(2)}) copy-start(f32[1536]{0:T(1024)} %param.16) | copy-start | bytes 18436
  330.6 72.2 %copy-start.1 = (bf16[384,1536]{1,0:T(8,128)(2,1)S(1)}, bf16[384,1536]{1,0:T(8,128)(2,1)}, u32[]{:S(2)}) copy-start(bf16[384,1536]{1,0:T(8,128)(2,1)} %param.13) | copy-start | bytes 3538948
  (14 other events, 26.4 us)
Sparse Core Ops, SparseCore 0:
  11.7 33.8 reduce-scatter.2
  48.9 38.7 all-gather.1
  330.7 69.7 reduce-scatter.4
where the time goes:
time: 411 us; the launch traced here: 409 us
  waiting for transfers between devices  241 us (59%)
  local copies, waits for them, and re-layouts  72 us (18%)
  other arithmetic  27 us (7%)
  matrix products  23.6 us (6%)
  starting transfers between devices  17 us (4%)
  blocking collectives  14.7 us (4%)
  between operations  14.4 us (4%)
    reduce_scatter x1, waiting for transfers between devices, on_device(): lax.psum_scatter(partial.reshape(n_exp * tok_rows, model_width), 'expert'...  69.9 us
    all_to_all x1, waiting for transfers between devices, on_device(): y_recv = lax.all_to_all(y_send, 'dp', 0, 0, tiled=True)  64.7 us
    all_to_all x1, waiting for transfers between devices, on_device(): lax.all_to_all(jnp.stack(weight_parts), 'dp', 0, 0, tiled=True)  57.2 us
    all_to_all x1, waiting for transfers between devices, on_device(): x_recv = lax.all_to_all(jnp.stack(x_parts), 'dp', 0, 0, tiled=True)  45.9 us
    another operation x18, local copies, waits for them, and re-layouts, as_rows(): return piece.reshape(-1, lane_width)  20.5 us
    unnamed x83, local copies, waits for them, and re-layouts  15.6 us
    all_gather x1, blocking collectives, on_device(): lax.all_gather(jnp.concatenate([expert_ids, replica_pick], axis=1), 'expe...  14.7 us
    slice x3, local copies, waits for them, and re-layouts, take(): piece = weight_recv[:, offset:offset + count].reshape((n_dp,) + shape)  8.72 us
  transfers between devices with their start and end apart: 6, of which 6 were waited for; matrix products, arithmetic and copies ran while one was open for 21% of the time, Pallas kernels for 0%

commit v1 on v0

--- a/solution.py
+++ b/solution.py
@@ -178,7 +178,19 @@
                 [slot_in[:, s] for s in owned_full[o]] + [slot_in[:, s] for s, _ in owned_part[o]]
             )
         )
-    x_recv = lax.all_to_all(jnp.stack(x_parts), "dp", 0, 0, tiled=True)
+    array = jnp.stack(x_parts)
+    ways, here_2 = (lax.axis_size("dp"), lax.axis_index("dp"))
+    width_2 = array.shape[0] // ways
+    dims = list(array.shape)
+    dims[0] = width_2
+    height = dims[0]
+    dims[0] = height * ways
+    x_recv = jnp.zeros(dims, array.dtype)
+    for mask in range(ways):
+        part_2 = lax.dynamic_slice_in_dim(array, (here_2 ^ mask) * width_2, width_2, axis=0)
+        if mask:
+            part_2 = lax.ppermute(part_2, "dp", [(d, d ^ mask) for d in range(ways)])
+        x_recv = lax.dynamic_update_slice_in_dim(x_recv, part_2, (here_2 ^ mask) * height, axis=0)
     unit_rows = n_dp * n_exp * CAP_MOST
 
     def expert_rows(rows, w_up, w_down, width):

time: 411 us -> 426 us (1.036)
  local copies, waits for them, and re-layouts: 72 us -> 85.4 us
  waiting for transfers between devices: 241 us -> 250 us
  other arithmetic: 27 us -> 22.1 us
    all_to_all x1 -> x0, waiting for transfers between devices: 45.9 us -> none  [on_device(): x_recv = lax.all_to_all(jnp.stack(x_parts), 'dp', 0, 0, tiled=True)]
    ppermute x0 -> x3, waiting for transfers between devices: none -> 36.6 us  [on_device(): part_2 = lax.ppermute(part_2, 'dp', [(d, d ^ mask) for d in range(ways)])]
    reduce_scatter x1, waiting for transfers between devices: 2.73 us -> 27.1 us  [on_device(): lax.psum_scatter(jnp.dot(flat_context, w_proj, preferred_element_type=jnp...]
    dynamic_update_slice x0 -> x3, local copies, waits for them, and re-layouts: none -> 8.1 us  [on_device(): lax.dynamic_update_slice_in_dim(x_recv, part_2, (here_2 ^ mask) * height,...]
    unnamed x83 -> x99, local copies, waits for them, and re-layouts: 15.6 us -> 9.76 us
    all_to_all x1 -> x0, starting transfers between devices: 5.54 us -> none  [on_device(): x_recv = lax.all_to_all(jnp.stack(x_parts), 'dp', 0, 0, tiled=True)]
    all_to_all x1, waiting for transfers between devices: 57.2 us -> 52.1 us  [on_device(): lax.all_to_all(jnp.stack(weight_parts), 'dp', 0, 0, tiled=True)]
  transfers between devices with their start and end apart: 6 -> 8, of which waited for: 6 -> 6; matrix products, arithmetic and copies ran while one was open for 21% -> 21% of each run, Pallas kernels for 0% -> 0%
where the time goes in v1:
time: 426 us; the launch traced here: 425 us
  waiting for transfers between devices  250 us (59%)
  local copies, waits for them, and re-layouts  85.4 us (20%)
  matrix products  23.8 us (6%)
  other arithmetic  22.1 us (5%)
  starting transfers between devices  15 us (4%)
  between operations  14.4 us (3%)
  blocking collectives  14.2 us (3%)
    reduce_scatter x1, waiting for transfers between devices, on_device(): lax.psum_scatter(partial.reshape(n_exp * tok_rows, model_width), 'expert'...  69.9 us
    all_to_all x1, waiting for transfers between devices, on_device(): y_recv = lax.all_to_all(y_send, 'dp', 0, 0, tiled=True)  64.5 us
    all_to_all x1, waiting for transfers between devices, on_device(): lax.all_to_all(jnp.stack(weight_parts), 'dp', 0, 0, tiled=True)  52.1 us
    ppermute x3, waiting for transfers between devices, on_device(): part_2 = lax.ppermute(part_2, 'dp', [(d, d ^ mask) for d in range(ways)])  36.6 us
    reduce_scatter x1, waiting for transfers between devices, on_device(): lax.psum_scatter(jnp.dot(flat_context, w_proj, preferred_element_type=jnp...  27.1 us
    another operation x18, local copies, waits for them, and re-layouts, as_rows(): return piece.reshape(-1, lane_width)  23.2 us
    all_gather x1, blocking collectives, on_device(): lax.all_gather(jnp.concatenate([expert_ids, replica_pick], axis=1), 'expe...  14.2 us
    unnamed x99, local copies, waits for them, and re-layouts  9.76 us
  transfers between devices with their start and end apart: 8, of which 6 were waited for; matrix products, arithmetic and copies ran while one was open for 21% of the time, Pallas kernels for 0%

profile of v1, /device:TPU:0, one launch (start us, length us, event | category | flops | bytes accessed | tf_op | source)
XLA Modules:
  0.0 425.0 jit_solution(10567164242771093573)
XLA Ops:
  8.4 3.3 convolution_convert_fusion.3
  13.3 3.2 fusion.61
  18.7 27.1 %reduce-scatter.3.cloned.1.call-done = bf16[128,1536]{1,0:T(8,128)(2,1)} async-done(((bf16[512,1536]{1,0:T(8,128)(2,1)}), bf16[128,1536]{1,0:T(8,128)(2,1)}) %reduce-scatter.3.cloned.1.call-update) | async-done | bytes 393232 | tf_op jit(solution)/shard_map/reduce_scatter | solution.py:142
  76.2 3.7 pad_maximum_fusion
  79.9 5.7 %all-to-all-start = ((bf16[4,1920,512]{2,1,0:T(8,128)(2,1)}), bf16[4,1920,512]{2,1,0:T(8,128)(2,1)}, u32[]{:S(2)}, u32[]{:S(2)}) async-start(bf16[4,1920,512]{2,1,0:T(8,128)(2,1)} %pad_maximum_fusion), calls=%async_computation.1 | async-start | bytes 15728640 | tf_op jit(solution)/shard_map/all_to_all | solution.py:117
  85.7 14.2 %all_gather.6 = s32[1024,16]{0,1:T(8,128)S(1)} all-gather(s32[128,16]{0,1:T(8,128)S(1)} %pad_add_fusion), channel_id=1, replica_groups=mesh['dp'=4,'expert'=8] {'expert'}, dimensions={0}, use_global_device_ids=true | all-gather | bytes 73728 | tf_op jit(solution)/shard_map/all_gather | solution.py:138
  106.7 3.3 convolution_convert_fusion
  112.1 3.4 broadcast_in_dim.91
  121.7 52.1 %all-to-all-done = bf16[4,1920,512]{2,1,0:T(8,128)(2,1)} async-done(((bf16[4,1920,512]{2,1,0:T(8,128)(2,1)}), bf16[4,1920,512]{2,1,0:T(8,128)(2,1)}, u32[]{:S(2)}, u32[]{:S(2)}) %all-to-all-start) | async-done | bytes 7864352 | tf_op jit(solution)/shard_map/all_to_all | solution.py:117
  173.7 3.8 slice.193
  177.6 5.6 %reshape_reshape.6 = bf16[1536,1024]{1,0:T(8,128)(2,1)} reshape(bf16[4,768,512]{2,1,0:T(8,128)(2,1)} %slice.193) | data formatting | bytes 6291456 | tf_op jit(solution)/shard_map/reshape;reshape | solution.py:129
  183.2 3.4 fusion.57
  186.6 3.7 reshape_reshape.7
  198.7 8.7 %collective-permute-done = bf16[1,2,8,32,1536]{4,3,2,1,0:T(8,128)(2,1)} collective-permute-done((bf16[1,2,8,32,1536]{4,3,2,1,0:T(8,128)(2,1)}, bf16[1,2,8,32,1536]{4,3,2,1,0:T(8,128)(2,1)}, u32[]{:S(2)}, u32[]{:S(2)}) %collective-permute-start) | collective-permute-done | bytes 1572896 | tf_op jit(solution)/shard_map/ppermute | solution.py:192
  207.4 2.7 constant_dynamic-update-slice_fusion.22
  212.8 27.9 %collective-permute-done.2 = bf16[1,2,8,32,1536]{4,3,2,1,0:T(8,128)(2,1)} collective-permute-done((bf16[1,2,8,32,1536]{4,3,2,1,0:T(8,128)(2,1)}, bf16[1,2,8,32,1536]{4,3,2,1,0:T(8,128)(2,1)}, u32[]{:S(2)}, u32[]{:S(2)}) %collective-permute-start.2) | collective-permute-done | bytes 1572896 | tf_op jit(solution)/shard_map/ppermute | solution.py:192
  243.5 3.4 fusion.59
  247.2 3.4 fusion.64
  255.3 3.2 maximum_bitcast_fusion
  258.5 5.4 %all-to-all-start.1 = ((bf16[4,2,8,32,1536]{4,3,2,1,0:T(8,128)(2,1)}), bf16[4,2,8,32,1536]{4,3,2,1,0:T(8,128)(2,1)}, u32[]{:S(2)}, u32[]{:S(2)}) async-start(bf16[4,2,8,32,1536]{4,3,2,1,0:T(8,128)(2,1)} %maximum_bitcast_fusion), calls=%async_computation.2 | async-start | bytes 12582912 | tf_op jit(solution)/shard_map/all_to_all | solution.py:217
  264.2 2.9 convolution_bitcast_fusion
  268.6 64.5 %all-to-all-done.1 = bf16[4,2,8,32,1536]{4,3,2,1,0:T(8,128)(2,1)} async-done(((bf16[4,2,8,32,1536]{4,3,2,1,0:T(8,128)(2,1)}), bf16[4,2,8,32,1536]{4,3,2,1,0:T(8,128)(2,1)}, u32[]{:S(2)}, u32[]{:S(2)}) %all-to-all-start.1) | async-done | bytes 6291488 | tf_op jit(solution)/shard_map/all_to_all | solution.py:217
  342.5 3.7 convolution_add_fusion
  346.3 69.9 %reduce-scatter.5.cloned.1.call-done = f32[128,1536]{1,0:T(8,128)} async-done(((f32[1024,1536]{1,0:T(8,128)}), f32[128,1536]{1,0:T(8,128)}) %reduce-scatter.5.cloned.1.call-update) | async-done | bytes 786448 | tf_op jit(solution)/shard_map/reduce_scatter | solution.py:236
  (182 shorter events, 82.4 us)
Async XLA Ops:
  7.2 38.6 %reduce-scatter.3.cloned.1.call-start = ((), (), s32[]{:S(2)}) async-start(), calls=%async_computation.4 | async-start | bytes 1966080 | tf_op jit(solution)/shard_map/reduce_scatter | solution.py:142
  11.8 94.9 %all-gather.2.cloned.1.call-start = ((), (), s32[]{:S(2)}) async-start(), calls=%async_computation.5 | async-start | bytes 3538944 | tf_op jit(solution)/shard_map/all_gather | solution.py:152
  13.3 32.5 %copy-start.2 = (bf16[128,1536]{1,0:T(8,128)(2,1)S(1)}, bf16[128,1536]{1,0:T(8,128)(2,1)}, u32[]{:S(2)}) copy-start(bf16[128,1536]{1,0:T(8,128)(2,1)} %param.14) | copy-start | bytes 1179652
  16.6 30.4 %copy-start.34 = (f32[1536]{0:T(1024)S(1)}, f32[1536]{0:T(1024)}, u32[]{:S(2)}) copy-start(f32[1536]{0:T(1024)} %param.15) | copy-start | bytes 18436
  48.9 4.4 %copy-start.14 = (bf16[1,128,1536]{2,1,0:T(8,128)(2,1)S(1)}, bf16[1,128,1536]{2,1,0:T(8,128)(2,1)}, u32[]{:S(2)}) copy-start(bf16[1,128,1536]{2,1,0:T(8,128)(2,1)} %get-tuple-element.36) | copy-start | bytes 1179652
  54.3 8.2 %copy-start.13 = (bf16[1,128,1536]{2,1,0:T(8,128)(2,1)S(1)}, bf16[1,128,1536]{2,1,0:T(8,128)(2,1)}, u32[]{:S(2)}) copy-start(bf16[1,128,1536]{2,1,0:T(8,128)(2,1)} %get-tuple-element.35) | copy-start | bytes 1179652
  58.8 7.5 %copy-start.12 = (bf16[1,128,1536]{2,1,0:T(8,128)(2,1)S(1)}, bf16[1,128,1536]{2,1,0:T(8,128)(2,1)}, u32[]{:S(2)}) copy-start(bf16[1,128,1536]{2,1,0:T(8,128)(2,1)} %get-tuple-element.38) | copy-start | bytes 1179652
  63.4 5.0 %copy-start.22 = (bf16[1,384,256]{2,1,0:T(8,128)(2,1)S(1)}, bf16[1,384,256]{2,1,0:T(8,128)(2,1)}, u32[]{:S(2)}) copy-start(bf16[1,384,256]{2,1,0:T(8,128)(2,1)} %get-tuple-element.29) | copy-start | bytes 589828
  64.6 4.6 %copy-start.21 = (bf16[1,384,256]{2,1,0:T(8,128)(2,1)S(1)}, bf16[1,384,256]{2,1,0:T(8,128)(2,1)}, u32[]{:S(2)}) copy-start(bf16[1,384,256]{2,1,0:T(8,128)(2,1)} %get-tuple-element.23) | copy-start | bytes 589828
  64.6 7.1 %copy-start.11 = (bf16[1,128,1536]{2,1,0:T(8,128)(2,1)S(1)}, bf16[1,128,1536]{2,1,0:T(8,128)(2,1)}, u32[]{:S(2)}) copy-start(bf16[1,128,1536]{2,1,0:T(8,128)(2,1)} %get-tuple-element.39) | copy-start | bytes 1179652
  67.2 5.4 %copy-start.5 = (bf16[768,512]{1,0:T(8,128)(2,1)S(1)}, bf16[768,512]{1,0:T(8,128)(2,1)}, u32[]{:S(2)}) copy-start(bf16[768,512]{1,0:T(8,128)(2,1)} %reshape_squeeze.63) | copy-start | bytes 2359300
  79.9 5.7 %copy-start.37 = (s32[128,8]{0,1:T(8,128)S(1)}, s32[128,8]{0,1:T(8,128)}, u32[]{:S(2)}) copy-start(s32[128,8]{0,1:T(8,128)} %param.19) | copy-start | bytes 12292
  79.9 5.7 %copy-start.38 = (s32[128,8]{0,1:T(8,128)S(1)}, s32[128,8]{0,1:T(8,128)}, u32[]{:S(2)}) copy-start(s32[128,8]{0,1:T(8,128)} %param.18) | copy-start | bytes 12292
  79.9 20.3 %copy-start.36 = (s32[48]{0:T(128)S(1)}, s32[48]{0:T(128)}, u32[]{:S(2)}) copy-start(s32[48]{0:T(128)} %param.20) | copy-start | bytes 580
  79.9 93.8 %all-to-all-start = ((bf16[4,1920,512]{2,1,0:T(8,128)(2,1)}), bf16[4,1920,512]{2,1,0:T(8,128)(2,1)}, u32[]{:S(2)}, u32[]{:S(2)}) async-start(bf16[4,1920,512]{2,1,0:T(8,128)(2,1)} %pad_maximum_fusion), calls=%async_computation.1 | async-start | bytes 15728640 | tf_op jit(solution)/shard_map/all_to_all | solution.py:117
  118.2 89.2 %collective-permute-start = (bf16[1,2,8,32,1536]{4,3,2,1,0:T(8,128)(2,1)}, bf16[1,2,8,32,1536]{4,3,2,1,0:T(8,128)(2,1)}, u32[]{:S(2)}, u32[]{:S(2)}) collective-permute-start(bf16[1,2,8,32,1536]{4,3,2,1,0:T(8,128)(2,1)} %get-tuple-element.14), channel_id=1, source_target_pairs={{0,8},{8,0},{16,24},{24,16},{1,9},{9,1},{17,25},{25,17},{2,10},{10... | collective-permute-start | bytes 4718600 | tf_op jit(solution)/shard_map/ppermute | solution.py:192
  120.2 90.0 %collective-permute-start.1 = (bf16[1,2,8,32,1536]{4,3,2,1,0:T(8,128)(2,1)}, bf16[1,2,8,32,1536]{4,3,2,1,0:T(8,128)(2,1)}, u32[]{:S(2)}, u32[]{:S(2)}) collective-permute-start(bf16[1,2,8,32,1536]{4,3,2,1,0:T(8,128)(2,1)} %get-tuple-element.13), channel_id=1, source_target_pairs={{0,16},{8,24},{16,0},{24,8},{1,17},{9,25},{17,1},{25,9},{2,18},{10... | collective-permute-start | bytes 4718600 | tf_op jit(solution)/shard_map/ppermute | solution.py:192
  121.7 119.1 %collective-permute-start.2 = (bf16[1,2,8,32,1536]{4,3,2,1,0:T(8,128)(2,1)}, bf16[1,2,8,32,1536]{4,3,2,1,0:T(8,128)(2,1)}, u32[]{:S(2)}, u32[]{:S(2)}) collective-permute-start(bf16[1,2,8,32,1536]{4,3,2,1,0:T(8,128)(2,1)} %get-tuple-element.12), channel_id=1, source_target_pairs={{0,24},{8,16},{16,8},{24,0},{1,25},{9,17},{17,9},{25,1},{2,26},{10... | collective-permute-start | bytes 4718600 | tf_op jit(solution)/shard_map/ppermute | solution.py:192
  258.5 5.7 %copy-start.33 = (bf16[1536,40]{0,1:T(8,128)(2,1)S(1)}, bf16[1536,40]{0,1:T(8,128)(2,1)}, u32[]{:S(2)}) copy-start(bf16[1536,40]{0,1:T(8,128)(2,1)} %param.17) | copy-start | bytes 368644
  258.5 74.5 %all-to-all-start.1 = ((bf16[4,2,8,32,1536]{4,3,2,1,0:T(8,128)(2,1)}), bf16[4,2,8,32,1536]{4,3,2,1,0:T(8,128)(2,1)}, u32[]{:S(2)}, u32[]{:S(2)}) async-start(bf16[4,2,8,32,1536]{4,3,2,1,0:T(8,128)(2,1)} %maximum_bitcast_fusion), calls=%async_computation.2 | async-start | bytes 12582912 | tf_op jit(solution)/shard_map/all_to_all | solution.py:217
  263.9 152.3 %reduce-scatter.5.cloned.1.call-start = ((), (), s32[]{:S(2)}) async-start(), calls=%async_computation.6 | async-start | bytes 7077888 | tf_op jit(solution)/shard_map/reduce_scatter | solution.py:236
  346.2 69.9 %copy-start.3 = (bf16[128,1536]{1,0:T(8,128)(2,1)S(1)}, bf16[128,1536]{1,0:T(8,128)(2,1)}, u32[]{:S(2)}) copy-start(bf16[128,1536]{1,0:T(8,128)(2,1)} %reduce-scatter.3.cloned.1.call-done) | copy-start | bytes 1179652
  346.3 71.3 %copy-start.35 = (f32[1536]{0:T(1024)S(1)}, f32[1536]{0:T(1024)}, u32[]{:S(2)}) copy-start(f32[1536]{0:T(1024)} %param.16) | copy-start | bytes 18436
  346.3 72.2 %copy-start.1 = (bf16[384,1536]{1,0:T(8,128)(2,1)S(1)}, bf16[384,1536]{1,0:T(8,128)(2,1)}, u32[]{:S(2)}) copy-start(bf16[384,1536]{1,0:T(8,128)(2,1)} %param.13) | copy-start | bytes 3538948
  (24 other events, 41.2 us)
Sparse Core Ops, SparseCore 0:
  11.9 33.8 reduce-scatter.2
  49.1 38.1 all-gather.1
  346.4 69.7 reduce-scatter.4
